TPU v7x, 128 devices: a whole 4x4x4 slice. The times are simulated.
128 devices in a mesh: seq: 32 (over x, y, core), fsdp: 4 (over z).
Axes of the slice: x: 4, y: 4, z: 4, core: 2. Of those that a mesh axis runs over, the one named last changes fastest.
Arguments:
- patches: bfloat16 [32768, 1280], P(('seq', 'fsdp')), may hold values from -6 to 6
- vis_index: int32 [32768], P(('seq', 'fsdp')), may hold values from 0 to 131071, as said below
- kv_list: int32 [256, 16], P(('seq', 'fsdp')), may hold values from 0 to 255, as said below
- kv_count: int32 [256], P(('seq', 'fsdp')), may hold values from 1 to 16, as said below
- global_tiles: int32 [2], replicated, may hold values from 0 to 255
- frame_table: bfloat16 [256, 1280], replicated, may hold values from -3 to 3
- space_table: bfloat16 [512, 1280], replicated, may hold values from -3 to 3
- ln_gain: bfloat16 [1280], replicated, may hold values from 0.25 to 1.75
- ln_bias: bfloat16 [1280], replicated, may hold values from -3 to 3
- w_qkv: bfloat16 [1280, 3840], P('fsdp')
- w_out: bfloat16 [1280, 1280], P('fsdp'), may hold values from -1.25 to 1.25
Outputs:
- attended: bfloat16 [32768, 1280], P(('seq', 'fsdp'))
Inputs may be any that keep to these rules, and one draw needn't show every extreme that they name: `vis_index`: exactly one visible position in each aligned group of four; strictly increasing. `kv_list`: the first entry of query tile i is i itself; entries may repeat; every entry t satisfies |t // 8 - i // 8| <= 2. Over all entries of an aligned run of 2 query tiles, the tiles that lie in any one group other than the run's own group (group = tile // 8) number at most 3 distinct ones, and exactly 3 for every such group within two of the run's own. On every device at least one query tile has kv_count = 16.
All inputs are finite; a program needn't handle non-finite values.
Results may differ from a plain program's by a relative error of at most 0.0065.
Values may be sent and summed in bfloat16 or wider, within the bound.
No kernel may reach another device: no remote copies, remote signals or barrier semaphores. Data moves between devices by JAX's collectives and lax.ppermute only.
A program may use at most 192 MiB of HBM per device.

v0:
```python
import jax
import jax.numpy as jnp
from jax import lax
from jax.sharding import PartitionSpec as P

HEADS = 16
TILE = 128
KT = 16
GLOBAL = 2
PATCHES = 512


def passed_along(block, axis, distance):
    devices = range(lax.axis_size(axis))
    route = [(i - distance, i) for i in devices if i - distance in devices]
    return lax.ppermute(block, axis, route)


def broadcast(shard, axis, root):
    mine = lax.axis_index(axis) == root
    return lax.psum(jnp.where(mine, shard, jnp.zeros_like(shard)), axis)


def layer_norm(stream, ln_gain, ln_bias):
    stream32 = stream.astype(jnp.float32)
    mean_val = jnp.mean(stream32, axis=-1, keepdims=True)
    centred = stream32 - mean_val
    variance = jnp.mean(centred * centred, axis=-1, keepdims=True)
    scaled = centred * lax.rsqrt(variance + 1e-06)
    return (scaled * ln_gain.astype(jnp.float32) + ln_bias.astype(jnp.float32)).astype(jnp.bfloat16)


def project(inputs, weight):
    return jnp.dot(
        inputs,
        lax.all_gather(weight, "fsdp", axis=0, tiled=True),
        preferred_element_type=jnp.float32,
    )


def attend_tile(query_tile, key_values, key_live, feat_width):
    head_size = feat_width // HEADS
    key_rows = key_values.shape[0]
    queries_h = query_tile.reshape(TILE, HEADS, head_size)
    keys_h = key_values[:, :feat_width].reshape(key_rows, HEADS, head_size)
    values_h = key_values[:, feat_width:].reshape(key_rows, HEADS, head_size)
    scores = jnp.einsum(
        "qhd,khd->hqk", queries_h, keys_h, preferred_element_type=jnp.float32
    ) * head_size ** (-0.5)
    scores = jnp.where(key_live[None, None, :], scores, -jnp.inf)
    row_max = jnp.max(scores, axis=-1, keepdims=True)
    weights_raw = jnp.exp(scores - row_max)
    probs = (weights_raw / jnp.sum(weights_raw, axis=-1, keepdims=True)).astype(jnp.bfloat16)
    mixed_h = jnp.einsum("hqk,khd->qhd", probs, values_h, preferred_element_type=jnp.float32)
    return mixed_h.reshape(TILE, feat_width).astype(jnp.bfloat16)


def local(
    patches,
    vis_index,
    kv_list,
    kv_count,
    global_tiles,
    frame_table,
    space_table,
    ln_gain,
    ln_bias,
    w_qkv,
    w_out,
):
    tok_rows = patches.shape[0]
    feat_width = patches.shape[1]
    tile_count = tok_rows // TILE
    frame_ids = vis_index // PATCHES
    patch_ids = vis_index % PATCHES
    stream = (
        patches.astype(jnp.float32)
        + frame_table[frame_ids].astype(jnp.float32)
        + space_table[patch_ids].astype(jnp.float32)
    ).astype(jnp.bfloat16)
    normed = layer_norm(stream, ln_gain, ln_bias)
    qkv = project(normed, w_qkv).astype(jnp.bfloat16)
    query = qkv[:, :feat_width]
    keyval = qkv[:, feat_width:]
    group_block = lax.all_gather(keyval, "fsdp", axis=0, tiled=True)
    group_tiles = group_block.shape[0] // TILE
    blocks = []
    for offset in (2, 1, 0, -1, -2):
        if offset == 0:
            blocks.append(group_block)
        else:
            blocks.append(passed_along(group_block, "seq", offset))
    window = jnp.concatenate(blocks, axis=0)
    tile_source = window.reshape(5 * group_tiles, TILE, 2 * feat_width)
    local_lists = kv_list - (lax.axis_index("seq") - 2) * group_tiles
    global_list = []
    for slot_no in range(GLOBAL):
        tile_id = global_tiles[slot_no]
        owner_index = tile_id // tile_count
        tile_piece = lax.dynamic_slice_in_dim(keyval, tile_id % tile_count * TILE, TILE, 0)
        global_list.append(broadcast(tile_piece, ("seq", "fsdp"), owner_index))
    global_kv = jnp.stack(global_list, axis=0)
    query_tiles = query.reshape(tile_count, TILE, feat_width)

    def per_tile(tile_args):
        query_tile, local_ids, live_count = tile_args
        slot_live_row = jnp.concatenate(
            [jnp.arange(KT) < live_count, jnp.ones((GLOBAL,), dtype=bool)]
        )
        key_live = jnp.repeat(slot_live_row, TILE)
        key_values = jnp.concatenate([tile_source[local_ids], global_kv], axis=0).reshape(
            (KT + GLOBAL) * TILE, 2 * feat_width
        )
        return attend_tile(query_tile, key_values, key_live, feat_width)

    heads_out = lax.map(per_tile, (query_tiles, local_lists, kv_count)).reshape(
        tok_rows, feat_width
    )
    return project(heads_out, w_out).astype(jnp.bfloat16)


def solution(mesh):
    return jax.shard_map(
        local,
        mesh=mesh,
        in_specs=(
            P(("seq", "fsdp"), None),
            P(("seq", "fsdp")),
            P(("seq", "fsdp"), None),
            P(("seq", "fsdp")),
            P(),
            P(),
            P(),
            P(),
            P(),
            P("fsdp", None),
            P("fsdp", None),
        ),
        out_specs=P(("seq", "fsdp"), None),
        check_vma=False,
    )
```

profile of v0, /device:TPU:1, one launch (start us, length us, event | category | flops | bytes accessed | tf_op | source)
XLA Modules:
  0.0 664.7 jit_solution(8370119231040135235)
XLA Ops:
  6.5 0.7 all-gather.4.cloned.1.call-update
  7.3 0.7 convert_element_type.54
  8.0 0.7 convert_element_type.55
  8.7 0.7 compare_select_fusion.2
  9.4 1.3 gather_fusion.1
  10.7 1.2 gather_fusion.2
  12.6 94.7 %all-gather.4.cloned.1.call-done = bf16[1280,3840]{1,0:T(8,128)(2,1)} async-done(((bf16[320,3840]{1,0:T(8,128)(2,1)}), bf16[1280,3840]{1,0:T(8,128)(2,1)}) %all-gather.4.cloned.1.call-update) | async-done | bytes 9830416 | tf_op jit(solution)/shard_map/all_gather | solution.py:36
  107.4 6.6 convolution_convert_fusion
  114.0 1.3 slice.30
  115.4 58.2 %all-gather.6.cloned.1.call-done = bf16[1024,2560]{1,0:T(8,128)(2,1)} async-done(((bf16[256,2560]{1,0:T(8,128)(2,1)}), bf16[1024,2560]{1,0:T(8,128)(2,1)}) %all-gather.6.cloned.1.call-update) | async-done | bytes 5242896 | tf_op jit(solution)/shard_map/all_gather | solution.py:85
  173.6 5.3 collective-permute-start
  178.9 1.9 collective-permute-start.1
  180.8 4.8 collective-permute-start.2
  185.6 1.3 collective-permute-start.3
  192.7 2.6 select_bitcast_fusion
  195.9 281.7 %all-reduce.4.cloned.1.call-done = (bf16[1,128,2560]{2,1,0:T(8,128)(2,1)}, bf16[1,128,2560]{2,1,0:T(8,128)(2,1)}) async-done(((bf16[1,128,2560]{2,1,0:T(8,128)(2,1)}, bf16[1,128,2560]{2,1,0:T(8,128)(2,1)}), (bf16[1,128,2560]{2,1,0:T(8,128)(2,1)}, bf16[1,128,2560]{2,1,0:T(8,128)(2,1)})) %all-reduce.4.cloned.1.call-update) | async-done | bytes 1310736 | tf_op jit(solution)/shard_map/psum | solution.py:21
  477.6 2.5 copy.23
  480.2 3.8 copy.24
  483.9 5.4 constant_dynamic-update-slice_fusion.5
  489.3 5.3 constant_dynamic-update-slice_fusion.4
  494.6 2.7 constant_dynamic-update-slice_fusion.3
  497.3 5.1 constant_dynamic-update-slice_fusion.2
  502.4 5.3 constant_dynamic-update-slice_fusion.1
  507.7 146.3 %while.10 = (s32[]{:T(128)}, bf16[2,128,1280]{2,1,0:T(8,128)(2,1)}, s32[2,16]{1,0:T(2,128)S(1)}, bf16[40,128,2560]{2,1,0:T(8,128)(2,1)}, bf16[1,128,2560]{1,0,2:...) while((s32[]{:T(128)}, bf16[2,128,1280]{2,1,0:T(8,128)(2,1)}, ...), condition=%wide.region_7.8_spmd, body=%wide.region_4.7_spmd.sunk | while | flops 1550224640 | bytes 152462336 | solution.py:116
  507.7 14.1 %gather_fusion = bf16[16,128,2560]{2,1,0:T(8,128)(2,1)} fusion(bf16[40,128,2560]{2,1,0:T(8,128)(2,1)} %get-tuple-element.176, s32[1024]{0:T(1024)S(1)} %pad_clamp_fusion.4), kind=kCustom, calls=%fused_computation.clone.1 | custom fusion | bytes 20971584 | tf_op jit(solution)/shard_map/while/body/eval_jaxpr/gather | solution.py:111
  521.9 2.5 copy.38
  524.4 0.9 copy.39
  525.3 7.8 %pad_maximum_fusion.2 = bf16[18,128,2560]{2,1,0:T(8,128)(2,1)S(1)} fusion(bf16[1,128,2560]{2,1,0:T(8,128)(2,1)S(1)} %copy.38, bf16[1,128,2560]{2,1,0:T(8,128)(2,1)S(1)} %copy.39, bf16[16,128,2560]{2,1,0:T(8,128)(2,1)} %gather_fusion), kind=kLoop, calls=%fused_computation.8.clone.1 | loop fusion | flops 11796480 | bytes 23592960 | tf_op jit(solution)/shard_map/while/body/eval_jaxpr/concatenate | solution.py:111
  533.1 4.7 fusion.46
  537.8 8.9 %copy.42 = bf16[2304,1280]{0,1:T(8,128)(2,1)} copy(bf16[2304,1280]{1,0:T(8,128)(2,1)} %get-tuple-element.150) | data formatting | bytes 11796480 | tf_op jit(solution)/shard_map/while
  546.9 0.6 dynamic_slice.35
  547.4 0.6 iota_compare_fusion.2
  548.2 11.2 %fusion.47 = (f32[16,128]{1,0:T(8,128)S(1)}, f32[16,128,2304]{2,1,0:T(8,128)}) fusion(pred[2304]{0:T(1024)(128)(4,1)S(1)} %broadcast_bitcast_fusion.2, bf16[128,16,80]{0,2,1:T(8,128)(2,1)S(1)} %bitcast.63, bf16[2304,16,80]{0,2,1:T(8,128)(2,1)} %bitcast.60), kind=kOutput, calls=%fused_computation.63.clone.1 | convolution fusion | flops 773851392 | bytes 25110784 | tf_op jit(solution)/shard_map/while/body/eval_jaxpr/sub | solution.py:52
  559.4 8.9 %copy.40 = bf16[2304,1280]{0,1:T(8,128)(2,1)} copy(bf16[2304,1280]{1,0:T(8,128)(2,1)} %get-tuple-element.149) | data formatting | bytes 11796480 | tf_op jit(solution)/shard_map/while
  568.2 11.6 %fusion.48 = bf16[16,80,128]{2,1,0:T(8,128)(2,1)S(1)} fusion(bf16[2304,16,80]{0,2,1:T(8,128)(2,1)} %bitcast.61, f32[16,128,2304]{2,1,0:T(8,128)} %get-tuple-element.151, f32[16,128]{1,0:T(8,128)S(1)} %get-tuple-element.152), kind=kOutput, calls=%fused_computation.14.clone.1 | convolution fusion | flops 764575744 | bytes 25108480 | tf_op jit(solution)/shard_map/while/body/eval_jaxpr/hqk,khd->qhd/dot_general | solution.py:54
  580.1 0.8 copy-done.8
  580.9 14.1 %gather_fusion = bf16[16,128,2560]{2,1,0:T(8,128)(2,1)} fusion(bf16[40,128,2560]{2,1,0:T(8,128)(2,1)} %get-tuple-element.176, s32[1024]{0:T(1024)S(1)} %pad_clamp_fusion.4), kind=kCustom, calls=%fused_computation.clone.1 | custom fusion | bytes 20971584 | tf_op jit(solution)/shard_map/while/body/eval_jaxpr/gather | solution.py:111
  595.0 2.5 copy.38
  597.5 0.9 copy.39
  598.4 7.8 %pad_maximum_fusion.2 = bf16[18,128,2560]{2,1,0:T(8,128)(2,1)S(1)} fusion(bf16[1,128,2560]{2,1,0:T(8,128)(2,1)S(1)} %copy.38, bf16[1,128,2560]{2,1,0:T(8,128)(2,1)S(1)} %copy.39, bf16[16,128,2560]{2,1,0:T(8,128)(2,1)} %gather_fusion), kind=kLoop, calls=%fused_computation.8.clone.1 | loop fusion | flops 11796480 | bytes 23592960 | tf_op jit(solution)/shard_map/while/body/eval_jaxpr/concatenate | solution.py:111
  606.2 4.7 fusion.46
  610.9 8.9 %copy.42 = bf16[2304,1280]{0,1:T(8,128)(2,1)} copy(bf16[2304,1280]{1,0:T(8,128)(2,1)} %get-tuple-element.150) | data formatting | bytes 11796480 | tf_op jit(solution)/shard_map/while
  620.6 0.6 iota_compare_fusion.2
  621.3 11.2 %fusion.47 = (f32[16,128]{1,0:T(8,128)S(1)}, f32[16,128,2304]{2,1,0:T(8,128)}) fusion(pred[2304]{0:T(1024)(128)(4,1)S(1)} %broadcast_bitcast_fusion.2, bf16[128,16,80]{0,2,1:T(8,128)(2,1)S(1)} %bitcast.63, bf16[2304,16,80]{0,2,1:T(8,128)(2,1)} %bitcast.60), kind=kOutput, calls=%fused_computation.63.clone.1 | convolution fusion | flops 773851392 | bytes 25110784 | tf_op jit(solution)/shard_map/while/body/eval_jaxpr/sub | solution.py:52
  632.5 8.9 %copy.40 = bf16[2304,1280]{0,1:T(8,128)(2,1)} copy(bf16[2304,1280]{1,0:T(8,128)(2,1)} %get-tuple-element.149) | data formatting | bytes 11796480 | tf_op jit(solution)/shard_map/while
  641.4 11.6 %fusion.48 = bf16[16,80,128]{2,1,0:T(8,128)(2,1)S(1)} fusion(bf16[2304,16,80]{0,2,1:T(8,128)(2,1)} %bitcast.61, f32[16,128,2304]{2,1,0:T(8,128)} %get-tuple-element.151, f32[16,128]{1,0:T(8,128)S(1)} %get-tuple-element.152), kind=kOutput, calls=%fused_computation.14.clone.1 | convolution fusion | flops 764575744 | bytes 25108480 | tf_op jit(solution)/shard_map/while/body/eval_jaxpr/hqk,khd->qhd/dot_general | solution.py:54
  653.2 0.8 copy-done.8
  654.1 4.1 convolution_convert_fusion.1
  (66 shorter events, 3.7 us)
Async XLA Ops:
  6.5 4.1 copy-start
  6.5 2.8 copy-start.2
  6.5 100.8 %all-gather.4.cloned.1.call-start = ((), (), s32[]{:S(2)}) async-start(), calls=%async_computation | async-start | bytes 12288000 | tf_op jit(solution)/shard_map/all_gather | solution.py:36
  7.3 166.3 %all-gather.6.cloned.1.call-start = ((), (), s32[]{:S(2)}) async-start(), calls=%async_computation.1 | async-start | bytes 6553600 | tf_op jit(solution)/shard_map/all_gather | solution.py:85
  9.4 2.5 copy-start.4
  12.6 174.3 %copy-start.5 = (s32[2]{0:T(128)S(1)}, s32[2]{0:T(128)}, u32[]{:S(2)}) copy-start(s32[2]{0:T(128)} %param.17) | copy-start | bytes 28
  114.0 363.6 %copy-start.3 = (bf16[256,3840]{1,0:T(8,128)(2,1)}, bf16[256,3840]{1,0:T(8,128)(2,1)S(1)}, u32[]{:S(2)}) copy-start(bf16[256,3840]{1,0:T(8,128)(2,1)S(1)} %convolution_convert_fusion) | copy-start | bytes 5898244
  114.0 81.8 %copy-start.6 = (s32[2,16]{1,0:T(2,128)S(1)}, s32[2,16]{1,0:T(2,128)}, u32[]{:S(2)}) copy-start(s32[2,16]{1,0:T(2,128)} %param.15) | copy-start | bytes 388
  115.3 362.3 %all-reduce.4.cloned.1.call-start = ((), (), s32[]{:S(2)}) async-start(), calls=%async_computation.3 | async-start | bytes 2621440 | tf_op jit(solution)/shard_map/psum | solution.py:21
  173.6 310.3 %collective-permute-start = (bf16[1024,2560]{1,0:T(8,128)(2,1)}, bf16[1024,2560]{1,0:T(8,128)(2,1)}, u32[]{:S(2)}, u32[]{:S(2)}) collective-permute-start(bf16[1024,2560]{1,0:T(8,128)(2,1)} %all-gather.6.cloned.1.call-done), channel_id=1, source_target_pairs={{0,8},{4,12},{8,16},{12,20},{16,24},{20,28},{24,32},{28,36},{32,40... | collective-permute-start | bytes 15728648 | tf_op jit(solution)/shard_map/ppermute | solution.py:16
  178.9 310.4 %collective-permute-start.1 = (bf16[1024,2560]{1,0:T(8,128)(2,1)}, bf16[1024,2560]{1,0:T(8,128)(2,1)}, u32[]{:S(2)}, u32[]{:S(2)}) collective-permute-start(bf16[1024,2560]{1,0:T(8,128)(2,1)} %all-gather.6.cloned.1.call-done), channel_id=1, source_target_pairs={{0,4},{4,8},{8,12},{12,16},{16,20},{20,24},{24,28},{28,32},{32,36}... | collective-permute-start | bytes 15728648 | tf_op jit(solution)/shard_map/ppermute | solution.py:16
  180.8 316.4 %collective-permute-start.2 = (bf16[1024,2560]{1,0:T(8,128)(2,1)}, bf16[1024,2560]{1,0:T(8,128)(2,1)}, u32[]{:S(2)}, u32[]{:S(2)}) collective-permute-start(bf16[1024,2560]{1,0:T(8,128)(2,1)} %all-gather.6.cloned.1.call-done), channel_id=1, source_target_pairs={{4,0},{8,4},{12,8},{16,12},{20,16},{24,20},{28,24},{32,28},{36,32}... | collective-permute-start | bytes 15728648 | tf_op jit(solution)/shard_map/ppermute | solution.py:16
  185.6 316.8 %collective-permute-start.3 = (bf16[1024,2560]{1,0:T(8,128)(2,1)}, bf16[1024,2560]{1,0:T(8,128)(2,1)}, u32[]{:S(2)}, u32[]{:S(2)}) collective-permute-start(bf16[1024,2560]{1,0:T(8,128)(2,1)} %all-gather.6.cloned.1.call-done), channel_id=1, source_target_pairs={{8,0},{12,4},{16,8},{20,12},{24,16},{28,20},{32,24},{36,28},{40,32... | collective-permute-start | bytes 15728648 | tf_op jit(solution)/shard_map/ppermute | solution.py:16
  195.3 458.8 %all-gather.8.cloned.1.call-start = ((), (), s32[]{:S(2)}) async-start(), calls=%async_computation.2 | async-start | bytes 4096000 | tf_op jit(solution)/shard_map/all_gather | solution.py:36
  483.9 10.7 %slice-start.1 = ((s8[5242880]{0:T(1024)(128)(4,1)}), s8[4194304]{0:T(1024)(128)(4,1)S(1)}, s32[]{:S(2)}) async-start(s8[5242880]{0:T(1024)(128)(4,1)} %bitcast.66), calls=%async_computation.5 | async-start | bytes 8388608
  489.3 5.3 slice-start.2
  502.4 5.3 slice-start
  502.4 5.3 copy-start.9
  568.2 11.8 %copy-start.7 = (bf16[2,128,1280]{2,1,0:T(8,128)(2,1)S(1)}, bf16[2,128,1280]{2,1,0:T(8,128)(2,1)}, u32[]{:S(2)}) copy-start(bf16[2,128,1280]{2,1,0:T(8,128)(2,1)} %get-tuple-element.164) | copy-start | bytes 1966084 | tf_op jit(solution)/shard_map/while
  580.1 0.8 copy-start.8
  641.4 11.8 %copy-start.7 = (bf16[2,128,1280]{2,1,0:T(8,128)(2,1)S(1)}, bf16[2,128,1280]{2,1,0:T(8,128)(2,1)}, u32[]{:S(2)}) copy-start(bf16[2,128,1280]{2,1,0:T(8,128)(2,1)} %get-tuple-element.164) | copy-start | bytes 1966084 | tf_op jit(solution)/shard_map/while
  653.2 0.8 copy-start.8
  654.1 4.1 copy-start.1
Sparse Core Ops, SparseCore 0:
  9.0 98.3 all-gather.3
  115.4 58.1 all-gather.5
  195.4 282.1 all-reduce.3
  479.1 39.0 all-gather.7
where the time goes:
time: 666 us; the launch traced here: 665 us
  waiting for transfers between devices  436 us (65%)
  local copies, waits for them, and re-layouts  118 us (18%)
  matrix products  56.3 us (8%)
  other arithmetic  22.2 us (3%)
  between operations  18.4 us (3%)
  starting transfers between devices  13.6 us (2%)
    psum x1, waiting for transfers between devices, broadcast(): return lax.psum(jnp.where(mine, shard, jnp.zeros_like(shard)), axis)  282 us
    all_gather x2, waiting for transfers between devices, project(): lax.all_gather(weight, 'fsdp', axis=0, tiled=True)  94.7 us
    all_gather x1, waiting for transfers between devices, local(): group_block = lax.all_gather(keyval, 'fsdp', axis=0, tiled=True)  58.2 us
    while x12, local copies, waits for them, and re-layouts  37.1 us
    gather x2, local copies, waits for them, and re-layouts, per_tile(): tile_source[local_ids]  28.2 us
    dot_general x2, matrix products, attend_tile(): jnp.einsum('hqk,khd->qhd', probs, values_h, preferred_element_type=jnp.fl...  23.2 us
    sub x2, matrix products, attend_tile(): weights_raw = jnp.exp(scores - row_max)  22.4 us
    unnamed x24, local copies, waits for them, and re-layouts  18.5 us
  transfers between devices with their start and end apart: 8, of which 3 were waited for; matrix products, arithmetic and copies ran while one was open for 28% of the time, Pallas kernels for 0%

commit v1 on v0

--- a/solution.py
+++ b/solution.py
@@ -82,7 +82,8 @@
     qkv = project(normed, w_qkv).astype(jnp.bfloat16)
     query = qkv[:, :feat_width]
     keyval = qkv[:, feat_width:]
-    group_block = lax.all_gather(keyval, "fsdp", axis=0, tiled=True)
+    stack = jnp.stack([keyval] * lax.axis_size("fsdp"))
+    group_block = jnp.concatenate(lax.all_to_all(stack, "fsdp", 0, 0), axis=0)
     group_tiles = group_block.shape[0] // TILE
     blocks = []
     for offset in (2, 1, 0, -1, -2):

time: 666 us -> 673 us (1.011)
  blocking collectives: 0 us -> 62.9 us
  waiting for transfers between devices: 436 us -> 378 us
    all_to_all x0 -> x1, blocking collectives: none -> 62.9 us  [local(): group_block = jnp.concatenate(lax.all_to_all(stack, 'fsdp', 0, 0), axis=0)]
    all_gather x1 -> x0, waiting for transfers between devices: 58.2 us -> none  [local(): group_block = lax.all_gather(keyval, 'fsdp', axis=0, tiled=True)]
    unnamed x24 -> x20, local copies, waits for them, and re-layouts: 18.5 us -> 20.8 us
  transfers between devices with their start and end apart: 8 -> 7, of which waited for: 3 -> 2; matrix products, arithmetic and copies ran while one was open for 28% -> 27% of each run, Pallas kernels for 0% -> 0%
where the time goes in v1:
time: 673 us; the launch traced here: 671 us
  waiting for transfers between devices  378 us (56%)
  local copies, waits for them, and re-layouts  120 us (18%)
  blocking collectives  62.9 us (9%)
  matrix products  56.4 us (8%)
  other arithmetic  20.9 us (3%)
  between operations  18.4 us (3%)
  starting transfers between devices  14.7 us (2%)
    psum x1, waiting for transfers between devices, broadcast(): return lax.psum(jnp.where(mine, shard, jnp.zeros_like(shard)), axis)  282 us
    all_gather x2, waiting for transfers between devices, project(): lax.all_gather(weight, 'fsdp', axis=0, tiled=True)  94.8 us
    all_to_all x1, blocking collectives, local(): group_block = jnp.concatenate(lax.all_to_all(stack, 'fsdp', 0, 0), axis=0)  62.9 us
    while x12, local copies, waits for them, and re-layouts  37 us
    gather x2, local copies, waits for them, and re-layouts, per_tile(): tile_source[local_ids]  28.1 us
    dot_general x2, matrix products, attend_tile(): jnp.einsum('hqk,khd->qhd', probs, values_h, preferred_element_type=jnp.fl...  23.2 us
    sub x2, matrix products, attend_tile(): weights_raw = jnp.exp(scores - row_max)  22.4 us
    unnamed x20, local copies, waits for them, and re-layouts  20.8 us
  transfers between devices with their start and end apart: 7, of which 2 were waited for; matrix products, arithmetic and copies ran while one was open for 27% of the time, Pallas kernels for 0%

profile of v1, /device:TPU:1, one launch (start us, length us, event | category | flops | bytes accessed | tf_op | source)
XLA Modules:
  0.0 670.8 jit_solution(18154443351513502548)
XLA Ops:
  6.5 0.7 all-gather.3.cloned.1.call-update
  7.3 0.7 convert_element_type.54
  8.0 0.7 convert_element_type.55
  8.7 0.7 compare_select_fusion.2
  9.4 1.3 gather_fusion.1
  10.7 1.2 gather_fusion.2
  12.6 94.7 %all-gather.3.cloned.1.call-done = bf16[1280,3840]{1,0:T(8,128)(2,1)} async-done(((bf16[320,3840]{1,0:T(8,128)(2,1)}), bf16[1280,3840]{1,0:T(8,128)(2,1)}) %all-gather.3.cloned.1.call-update) | async-done | bytes 9830416 | tf_op jit(solution)/shard_map/all_gather | solution.py:36
  107.4 6.6 convolution_convert_fusion
  114.6 62.9 %all_to_all.5 = bf16[4,256,2560]{2,1,0:T(8,128)(2,1)} all-to-all(bf16[4,256,2560]{2,1,0:T(8,128)(2,1)S(1)} %stack.6), channel_id=1, replica_groups=mesh['seq'=32,'fsdp'=4] {'fsdp'}, dimensions={0} | all-to-all | bytes 10485760 | tf_op jit(solution)/shard_map/all_to_all | solution.py:86
  177.5 5.4 collective-permute-start
  182.8 3.0 collective-permute-start.1
  185.8 4.8 collective-permute-start.2
  190.6 1.3 collective-permute-start.3
  197.7 1.3 select_bitcast_fusion
  199.8 281.8 %all-reduce.4.cloned.1.call-done = (bf16[1,128,2560]{2,1,0:T(8,128)(2,1)}, bf16[1,128,2560]{2,1,0:T(8,128)(2,1)}) async-done(((bf16[1,128,2560]{2,1,0:T(8,128)(2,1)}, bf16[1,128,2560]{2,1,0:T(8,128)(2,1)}), (bf16[1,128,2560]{2,1,0:T(8,128)(2,1)}, bf16[1,128,2560]{2,1,0:T(8,128)(2,1)})) %all-reduce.4.cloned.1.call-update) | async-done | bytes 1310736 | tf_op jit(solution)/shard_map/psum | solution.py:21
  481.6 2.5 copy.23
  484.1 3.8 copy.24
  487.8 5.1 constant_dynamic-update-slice_fusion.5
  493.0 5.3 constant_dynamic-update-slice_fusion.4
  498.3 5.2 constant_dynamic-update-slice_fusion.3
  503.6 5.1 constant_dynamic-update-slice_fusion.2
  508.7 5.3 constant_dynamic-update-slice_fusion.1
  514.0 146.2 %while.10 = (s32[]{:T(128)}, bf16[2,128,1280]{2,1,0:T(8,128)(2,1)}, s32[2,16]{1,0:T(2,128)S(1)}, bf16[40,128,2560]{2,1,0:T(8,128)(2,1)}, bf16[1,128,2560]{1,0,2:...) while((s32[]{:T(128)}, bf16[2,128,1280]{2,1,0:T(8,128)(2,1)}, ...), condition=%wide.region_7.8_spmd, body=%wide.region_4.7_spmd.sunk | while | flops 1550224640 | bytes 152462336 | solution.py:117
  514.0 14.1 %gather_fusion = bf16[16,128,2560]{2,1,0:T(8,128)(2,1)} fusion(bf16[40,128,2560]{2,1,0:T(8,128)(2,1)} %get-tuple-element.176, s32[1024]{0:T(1024)S(1)} %pad_clamp_fusion.4), kind=kCustom, calls=%fused_computation.clone.1 | custom fusion | bytes 20971584 | tf_op jit(solution)/shard_map/while/body/eval_jaxpr/gather | solution.py:112
  528.1 2.5 copy.38
  530.6 0.9 copy.39
  531.5 7.8 %pad_maximum_fusion.2 = bf16[18,128,2560]{2,1,0:T(8,128)(2,1)S(1)} fusion(bf16[1,128,2560]{2,1,0:T(8,128)(2,1)S(1)} %copy.38, bf16[1,128,2560]{2,1,0:T(8,128)(2,1)S(1)} %copy.39, bf16[16,128,2560]{2,1,0:T(8,128)(2,1)} %gather_fusion), kind=kLoop, calls=%fused_computation.8.clone.1 | loop fusion | flops 11796480 | bytes 23592960 | tf_op jit(solution)/shard_map/while/body/eval_jaxpr/concatenate | solution.py:112
  539.3 4.7 fusion.46
  543.9 8.8 %copy.42 = bf16[2304,1280]{0,1:T(8,128)(2,1)} copy(bf16[2304,1280]{1,0:T(8,128)(2,1)} %get-tuple-element.150) | data formatting | bytes 11796480 | tf_op jit(solution)/shard_map/while
  553.0 0.6 dynamic_slice.35
  553.6 0.6 iota_compare_fusion.2
  554.4 11.2 %fusion.47 = (f32[16,128]{1,0:T(8,128)S(1)}, f32[16,128,2304]{2,1,0:T(8,128)}) fusion(pred[2304]{0:T(1024)(128)(4,1)S(1)} %broadcast_bitcast_fusion.2, bf16[128,16,80]{0,2,1:T(8,128)(2,1)S(1)} %bitcast.64, bf16[2304,16,80]{0,2,1:T(8,128)(2,1)} %bitcast.61), kind=kOutput, calls=%fused_computation.63.clone.1 | convolution fusion | flops 773851392 | bytes 25110784 | tf_op jit(solution)/shard_map/while/body/eval_jaxpr/sub | solution.py:52
  565.6 8.8 %copy.40 = bf16[2304,1280]{0,1:T(8,128)(2,1)} copy(bf16[2304,1280]{1,0:T(8,128)(2,1)} %get-tuple-element.149) | data formatting | bytes 11796480 | tf_op jit(solution)/shard_map/while
  574.4 11.6 %fusion.48 = bf16[16,80,128]{2,1,0:T(8,128)(2,1)S(1)} fusion(bf16[2304,16,80]{0,2,1:T(8,128)(2,1)} %bitcast.62, f32[16,128,2304]{2,1,0:T(8,128)} %get-tuple-element.151, f32[16,128]{1,0:T(8,128)S(1)} %get-tuple-element.152), kind=kOutput, calls=%fused_computation.14.clone.1 | convolution fusion | flops 764575744 | bytes 25108480 | tf_op jit(solution)/shard_map/while/body/eval_jaxpr/hqk,khd->qhd/dot_general | solution.py:54
  586.3 0.8 copy-done.8
  587.1 14.1 %gather_fusion = bf16[16,128,2560]{2,1,0:T(8,128)(2,1)} fusion(bf16[40,128,2560]{2,1,0:T(8,128)(2,1)} %get-tuple-element.176, s32[1024]{0:T(1024)S(1)} %pad_clamp_fusion.4), kind=kCustom, calls=%fused_computation.clone.1 | custom fusion | bytes 20971584 | tf_op jit(solution)/shard_map/while/body/eval_jaxpr/gather | solution.py:112
  601.2 2.5 copy.38
  603.7 0.9 copy.39
  604.6 7.8 %pad_maximum_fusion.2 = bf16[18,128,2560]{2,1,0:T(8,128)(2,1)S(1)} fusion(bf16[1,128,2560]{2,1,0:T(8,128)(2,1)S(1)} %copy.38, bf16[1,128,2560]{2,1,0:T(8,128)(2,1)S(1)} %copy.39, bf16[16,128,2560]{2,1,0:T(8,128)(2,1)} %gather_fusion), kind=kLoop, calls=%fused_computation.8.clone.1 | loop fusion | flops 11796480 | bytes 23592960 | tf_op jit(solution)/shard_map/while/body/eval_jaxpr/concatenate | solution.py:112
  612.4 4.7 fusion.46
  617.0 8.8 %copy.42 = bf16[2304,1280]{0,1:T(8,128)(2,1)} copy(bf16[2304,1280]{1,0:T(8,128)(2,1)} %get-tuple-element.150) | data formatting | bytes 11796480 | tf_op jit(solution)/shard_map/while
  626.1 0.6 dynamic_slice.35
  626.7 0.6 iota_compare_fusion.2
  627.5 11.2 %fusion.47 = (f32[16,128]{1,0:T(8,128)S(1)}, f32[16,128,2304]{2,1,0:T(8,128)}) fusion(pred[2304]{0:T(1024)(128)(4,1)S(1)} %broadcast_bitcast_fusion.2, bf16[128,16,80]{0,2,1:T(8,128)(2,1)S(1)} %bitcast.64, bf16[2304,16,80]{0,2,1:T(8,128)(2,1)} %bitcast.61), kind=kOutput, calls=%fused_computation.63.clone.1 | convolution fusion | flops 773851392 | bytes 25110784 | tf_op jit(solution)/shard_map/while/body/eval_jaxpr/sub | solution.py:52
  638.7 8.8 %copy.40 = bf16[2304,1280]{0,1:T(8,128)(2,1)} copy(bf16[2304,1280]{1,0:T(8,128)(2,1)} %get-tuple-element.149) | data formatting | bytes 11796480 | tf_op jit(solution)/shard_map/while
  647.5 11.6 %fusion.48 = bf16[16,80,128]{2,1,0:T(8,128)(2,1)S(1)} fusion(bf16[2304,16,80]{0,2,1:T(8,128)(2,1)} %bitcast.62, f32[16,128,2304]{2,1,0:T(8,128)} %get-tuple-element.151, f32[16,128]{1,0:T(8,128)S(1)} %get-tuple-element.152), kind=kOutput, calls=%fused_computation.14.clone.1 | convolution fusion | flops 764575744 | bytes 25108480 | tf_op jit(solution)/shard_map/while/body/eval_jaxpr/hqk,khd->qhd/dot_general | solution.py:54
  659.4 0.8 copy-done.8
  660.2 4.1 convolution_convert_fusion.1
  (60 shorter events, 3.7 us)
Async XLA Ops:
  6.5 4.1 copy-start
  6.5 2.8 copy-start.2
  6.5 100.8 %all-gather.3.cloned.1.call-start = ((), (), s32[]{:S(2)}) async-start(), calls=%async_computation.1 | async-start | bytes 12288000 | tf_op jit(solution)/shard_map/all_gather | solution.py:36
  7.3 474.3 %all-reduce.4.cloned.1.call-start = ((), (), s32[]{:S(2)}) async-start(), calls=%async_computation.3 | async-start | bytes 2621440 | tf_op jit(solution)/shard_map/psum | solution.py:21
  9.4 2.5 copy-start.4
  114.0 85.7 %copy-start.3 = (bf16[256,3840]{1,0:T(8,128)(2,1)}, bf16[256,3840]{1,0:T(8,128)(2,1)S(1)}, u32[]{:S(2)}) copy-start(bf16[256,3840]{1,0:T(8,128)(2,1)S(1)} %convolution_convert_fusion) | copy-start | bytes 5898244
  114.5 77.4 %copy-start.5 = (s32[2]{0:T(128)S(1)}, s32[2]{0:T(128)}, u32[]{:S(2)}) copy-start(s32[2]{0:T(128)} %param.17) | copy-start | bytes 28
  114.5 85.2 %copy-start.6 = (s32[2,16]{1,0:T(2,128)S(1)}, s32[2,16]{1,0:T(2,128)}, u32[]{:S(2)}) copy-start(s32[2,16]{1,0:T(2,128)} %param.15) | copy-start | bytes 388
  177.5 310.4 %collective-permute-start = (bf16[1024,2560]{1,0:T(8,128)(2,1)}, bf16[1024,2560]{1,0:T(8,128)(2,1)}, u32[]{:S(2)}, u32[]{:S(2)}) collective-permute-start(bf16[1024,2560]{1,0:T(8,128)(2,1)} %bitcast.10), channel_id=1, source_target_pairs={{0,8},{4,12},{8,16},{12,20},{16,24},{20,28},{24,32},{28,36},{32,40... | collective-permute-start | bytes 15728648 | tf_op jit(solution)/shard_map/ppermute | solution.py:16
  182.8 310.2 %collective-permute-start.1 = (bf16[1024,2560]{1,0:T(8,128)(2,1)}, bf16[1024,2560]{1,0:T(8,128)(2,1)}, u32[]{:S(2)}, u32[]{:S(2)}) collective-permute-start(bf16[1024,2560]{1,0:T(8,128)(2,1)} %bitcast.10), channel_id=1, source_target_pairs={{0,4},{4,8},{8,12},{12,16},{16,20},{20,24},{24,28},{28,32},{32,36}... | collective-permute-start | bytes 15728648 | tf_op jit(solution)/shard_map/ppermute | solution.py:16
  185.8 317.7 %collective-permute-start.2 = (bf16[1024,2560]{1,0:T(8,128)(2,1)}, bf16[1024,2560]{1,0:T(8,128)(2,1)}, u32[]{:S(2)}, u32[]{:S(2)}) collective-permute-start(bf16[1024,2560]{1,0:T(8,128)(2,1)} %bitcast.10), channel_id=1, source_target_pairs={{4,0},{8,4},{12,8},{16,12},{20,16},{24,20},{28,24},{32,28},{36,32}... | collective-permute-start | bytes 15728648 | tf_op jit(solution)/shard_map/ppermute | solution.py:16
  190.6 318.0 %collective-permute-start.3 = (bf16[1024,2560]{1,0:T(8,128)(2,1)}, bf16[1024,2560]{1,0:T(8,128)(2,1)}, u32[]{:S(2)}, u32[]{:S(2)}) collective-permute-start(bf16[1024,2560]{1,0:T(8,128)(2,1)} %bitcast.10), channel_id=1, source_target_pairs={{8,0},{12,4},{16,8},{20,12},{24,16},{28,20},{32,24},{36,28},{40,32... | collective-permute-start | bytes 15728648 | tf_op jit(solution)/shard_map/ppermute | solution.py:16
  199.0 461.2 %all-gather.5.cloned.1.call-start = ((), (), s32[]{:S(2)}) async-start(), calls=%async_computation.2 | async-start | bytes 4096000 | tf_op jit(solution)/shard_map/all_gather | solution.py:36
  508.7 5.3 slice-start
  508.7 5.3 copy-start.9
  574.4 11.8 %copy-start.7 = (bf16[2,128,1280]{2,1,0:T(8,128)(2,1)S(1)}, bf16[2,128,1280]{2,1,0:T(8,128)(2,1)}, u32[]{:S(2)}) copy-start(bf16[2,128,1280]{2,1,0:T(8,128)(2,1)} %get-tuple-element.164) | copy-start | bytes 1966084 | tf_op jit(solution)/shard_map/while
  586.3 0.8 copy-start.8
  647.5 11.8 %copy-start.7 = (bf16[2,128,1280]{2,1,0:T(8,128)(2,1)S(1)}, bf16[2,128,1280]{2,1,0:T(8,128)(2,1)}, u32[]{:S(2)}) copy-start(bf16[2,128,1280]{2,1,0:T(8,128)(2,1)} %get-tuple-element.164) | copy-start | bytes 1966084 | tf_op jit(solution)/shard_map/while
  659.4 0.8 copy-start.8
  660.2 4.1 copy-start.1
Sparse Core Ops, SparseCore 0:
  9.0 98.3 all-gather.2
  199.1 282.4 all-reduce.3
  483.2 39.0 all-gather.4
